TPU v7x, 256 devices: a whole 4x4x8 slice. The times are simulated.
256 devices in a mesh: samp: 64 (over x, z, core), blk: 4 (over y).
Axes of the slice: x: 4, y: 4, z: 8, core: 2. Of those that a mesh axis runs over, the one named last changes fastest.
Arguments:
- dosages: bfloat16 [40960, 2048], P('samp', 'blk'), may hold values from 0 to 2
- traits: bfloat16 [16, 40960], P(None, 'samp'), may hold values from -6 to 6
- folds: int32 [40960], P('samp'), may hold values from 0 to 4
Outputs:
- level0: float32 [4, 5, 16, 40960], P(None, None, 'blk', 'samp')
- blend: float32 [16, 40960], P('blk', 'samp')
All inputs are finite; a program needn't handle non-finite values.
Results may differ from a plain program's by a relative error of at most 0.0097.
Values may be sent and summed in bfloat16 or wider, within the bound.
No kernel may reach another device: no remote copies, remote signals or barrier semaphores. Data moves between devices by JAX's collectives and lax.ppermute only.
A program may use at most 64 MiB of HBM per device.

v0:
```python
import jax
import jax.numpy as jnp
import numpy as np
from jax import lax
from jax.sharding import Mesh
from jax.sharding import PartitionSpec as P

FOLDS = 5
SHRINK = 5
RATIOS = (99.0, 3.0, 1.0, 1.0 / 3.0, 1.0 / 99.0)
EPS = 1e-05
HIGH = lax.Precision.HIGHEST
SAMP = ("x", "z", "c")


def solve_batch(systems, right_sides):
    factors = jnp.linalg.cholesky(systems)

    def solve_single(factor, right_side):
        return jax.scipy.linalg.cho_solve((factor, True), right_side)

    return jax.vmap(solve_single)(factors, right_sides)


def psum_tree(value):
    for name in ("c", "z", "x"):
        value = lax.psum(value, name)
    return value


def shards(dosages, traits, folds):
    rows, width = dosages.shape
    traits_count = traits.shape[0]
    fold_ids = jnp.arange(FOLDS, dtype=jnp.int32)
    masks = (folds[None, :] == fold_ids[:, None]).astype(jnp.float32)
    mask_half = masks.astype(jnp.bfloat16)
    traits_wide = traits.astype(jnp.float32)
    augmented = jnp.concatenate([dosages, jnp.ones((rows, 1), jnp.bfloat16), traits.T], axis=1)
    weighted = mask_half[:, :, None] * augmented[None]
    stats = jnp.einsum("ri,krj->kij", augmented, weighted, preferred_element_type=jnp.float32)
    stats = lax.psum(stats, SAMP)
    gram = stats[:, :width, :width]
    sums = stats[:, :width, width]
    counts = stats[:, width, width]
    cross = stats[:, width + 1 :, :width]
    trait_sums = stats[:, width + 1 :, width]
    total = jnp.sum(counts)
    mean = jnp.sum(sums, axis=0) / total
    gram_total = jnp.sum(gram, axis=0)
    variance = jnp.diagonal(gram_total) / total - mean * mean
    scale = lax.rsqrt(variance + EPS)
    sums_total = jnp.sum(sums, axis=0)
    cross_total = jnp.sum(cross, axis=0)
    trait_total = jnp.sum(trait_sums, axis=0)
    ratios = jnp.array(RATIOS, dtype=jnp.float32)
    identity = jnp.eye(width, dtype=jnp.float32)

    def train_system(fold):
        train_gram = gram_total - lax.dynamic_index_in_dim(gram, fold, 0, keepdims=False)
        train_sums = sums_total - lax.dynamic_index_in_dim(sums, fold, 0, keepdims=False)
        train_count = total - lax.dynamic_index_in_dim(counts, fold, 0, keepdims=False)
        train_cross = cross_total - lax.dynamic_index_in_dim(cross, fold, 0, keepdims=False)
        train_traits = trait_total - lax.dynamic_index_in_dim(trait_sums, fold, 0, keepdims=False)
        centered = (
            train_gram
            - mean[:, None] * train_sums[None, :]
            - train_sums[:, None] * mean[None, :]
            + train_count * mean[:, None] * mean[None, :]
        )
        system = scale[:, None] * centered * scale[None, :]
        target = scale[:, None] * (train_cross.T - mean[:, None] * train_traits[None, :])
        return (system, target)

    systems_count = FOLDS * SHRINK
    samp_size = lax.axis_size(SAMP)
    per_device = -(-systems_count // samp_size)
    first = lax.axis_index(SAMP) * per_device

    def solve_own(offset):
        which = jnp.minimum(first + offset, systems_count - 1)
        fold = which // SHRINK
        shrink = which - fold * SHRINK
        system, target = train_system(fold)
        penalty = jnp.sum(
            jnp.where(jnp.arange(SHRINK, dtype=jnp.int32) == shrink, ratios * width, 0.0)
        )
        beta = solve_batch((system + penalty * identity)[None], target[None])[0]
        return (scale[:, None] * beta).astype(jnp.bfloat16)

    owned = lax.map(solve_own, jnp.arange(per_device, dtype=jnp.int32))
    collected = lax.all_gather(owned, SAMP, axis=0, tiled=True)
    coef = collected[:systems_count].reshape(FOLDS, SHRINK, width, traits_count)
    coef_flat = coef.transpose(2, 0, 1, 3).reshape(width, FOLDS * SHRINK * traits_count)
    shift = jnp.einsum("v,klvt->klt", mean, coef.astype(jnp.float32), precision=HIGH)
    raw = jnp.einsum("vc,rv->cr", coef_flat, dosages, preferred_element_type=jnp.float32)
    outcome = raw.reshape(FOLDS, SHRINK, traits_count, rows) - shift[..., None]
    level_pred = jnp.einsum("kltr,kr->ltr", outcome, masks, precision=HIGH)
    group = traits_count // lax.axis_size("blk")
    start = lax.axis_index("blk") * group
    own_traits = lax.dynamic_slice_in_dim(traits_wide, start, group, 0)
    own_sums = lax.dynamic_slice_in_dim(trait_sums, start, group, 1)
    arrived = lax.all_to_all(level_pred[None], "blk", split_axis=2, concat_axis=0, tiled=True)
    count_pred = arrived.shape[0] * arrived.shape[1]
    flat = arrived.reshape(count_pred, group, rows)
    raw_grams = jnp.einsum("ks,ats,bts->ktab", masks, flat, flat, precision=HIGH)
    raw_sums = jnp.einsum("ks,ats->kta", masks, flat, precision=HIGH)
    raw_cross = jnp.einsum("ks,ats,ts->kta", masks, flat, own_traits, precision=HIGH)
    packed = jnp.concatenate(
        [
            raw_grams.reshape(FOLDS * group, count_pred * count_pred),
            raw_sums.reshape(FOLDS * group, count_pred),
            raw_cross.reshape(FOLDS * group, count_pred),
        ],
        axis=1,
    )
    packed = psum_tree(packed)
    raw_grams = packed[:, : count_pred * count_pred].reshape(FOLDS, group, count_pred, count_pred)
    raw_sums = packed[:, count_pred * count_pred : count_pred * (count_pred + 1)].reshape(
        FOLDS, group, count_pred
    )
    raw_cross = packed[:, count_pred * (count_pred + 1) :].reshape(FOLDS, group, count_pred)
    pred_sum = jnp.sum(raw_sums, axis=0)
    pred_sq = jnp.sum(jnp.diagonal(raw_grams, axis1=2, axis2=3), axis=0)
    pred_mean = pred_sum / total
    pred_var = pred_sq / total - pred_mean * pred_mean
    pred_scale = lax.rsqrt(pred_var + EPS)
    level0 = (flat - pred_mean.T[:, :, None]) * pred_scale.T[:, :, None]
    fold_mean = pred_mean[None]
    fold_sums = (raw_sums - counts[:, None, None] * fold_mean) * pred_scale[None]
    fold_grams = (
        raw_grams
        - fold_mean[..., :, None] * raw_sums[..., None, :]
        - raw_sums[..., :, None] * fold_mean[..., None, :]
        + counts[:, None, None, None] * fold_mean[..., :, None] * fold_mean[..., None, :]
    ) * (pred_scale[None, :, :, None] * pred_scale[None, :, None, :])
    fold_cross = (raw_cross - fold_mean * own_sums[:, :, None]) * pred_scale[None]
    level0 = level0.reshape(arrived.shape)
    train_grams = jnp.sum(fold_grams, axis=0)[None] - fold_grams
    train_cross = jnp.sum(fold_cross, axis=0)[None] - fold_cross
    shrunk = train_grams + total / 4.0 * jnp.eye(count_pred, dtype=jnp.float32)
    weights = solve_batch(
        shrunk.reshape(-1, count_pred, count_pred), train_cross.reshape(-1, count_pred)
    )
    weights = weights.reshape(FOLDS, group, count_pred)
    every_fold = jnp.einsum("ats,kta->kts", level0.reshape(flat.shape), weights, precision=HIGH)
    blended = jnp.einsum("kts,ks->ts", every_fold, masks, precision=HIGH)
    blend_sum = jnp.einsum("kta,kta->t", weights, fold_sums, precision=HIGH)
    blend_sq = jnp.einsum("kta,ktab,ktb->t", weights, fold_grams, weights, precision=HIGH)
    blend_mean = blend_sum / total
    blend_var = blend_sq / total - blend_mean * blend_mean
    blend = (blended - blend_mean[:, None]) * lax.rsqrt(blend_var + EPS)[:, None]
    return (level0, blend)


def view_of(mesh):
    devices = np.asarray(mesh.devices)
    samp, blk = devices.shape
    flat = list(devices.reshape(-1))
    xs = sorted({d.coords[0] for d in flat})
    zs = sorted({d.coords[2] for d in flat})
    cores = samp // (len(xs) * len(zs))
    view = devices.reshape(len(xs), len(zs), cores, blk)
    for (i, j, c, b), d in np.ndenumerate(view):
        assert d.coords[0] == xs[i] and d.coords[2] == zs[j]
    return Mesh(view, ("x", "z", "c", "blk"))


def solution(mesh):
    view = view_of(mesh)
    in_specs = (P(SAMP, "blk"), P(None, SAMP), P(SAMP))
    out_specs = (P(None, None, "blk", SAMP), P("blk", SAMP))
    return jax.shard_map(shards, mesh=view, in_specs=in_specs, out_specs=out_specs, check_vma=False)
```

profile of v0, /device:TPU:8, one launch (start us, length us, event | category | flops | bytes accessed | tf_op | source)
XLA Modules:
  0.0 606.8 jit_solution(15835812869913055414)
XLA Ops:
  7.2 1.4 copy.176
  8.6 1.3 convert_bitcast_fusion
  9.9 0.9 pad_maximum_fusion
  10.8 5.5 fusion.2
  16.5 0.5 copy-done.4
  17.0 0.6 fusion.97
  17.6 203.9 %all-reduce.3.cloned.1.call-done = f32[5,529,529]{1,2,0:T(8,128)} async-done(((f32[5,529,529]{1,2,0:T(8,128)}), f32[5,529,529]{1,2,0:T(8,128)}) %all-reduce.3.cloned.1.call-update) | async-done | bytes 5596836 | tf_op jit(solution)/shard_map/psum | solution.py:41
  221.5 1.5 slice_reduce_fusion.1
  223.0 0.5 constant_dynamic-slice_fusion.5
  223.5 0.9 fusion.108
  225.6 6.1 %fusion.109 = (f32[5,512,512]{1,2,0:T(8,128)}, f32[512,512]{0,1:T(8,128)S(1)}) fusion(f32[5,529,529]{1,2,0:T(8,128)} %all-reduce.3.cloned.1.call-done), kind=kLoop, calls=%fused_computation.227 | loop fusion | flops 1048576 | bytes 11534336 | tf_op jit(solution)/shard_map/slice | solution.py:42
  231.7 5.1 gather_fusion
  236.7 0.6 broadcast_multiply_fusion.3
  237.4 0.6 add_rsqrt_fusion.1
  238.0 2.4 fusion.35
  240.9 11.7 %custom-call.57 = f32[1,128,128]{2,1,0:T(8,128)S(1)} custom-call(f32[1,128,128]{2,1,0:T(8,128)S(1)} %cholesky.302), custom_call_target="Cholesky" | custom-call | tf_op jit(solution)/shard_map/while/body/eval_jaxpr/jit(cholesky)/cholesky | solution.py:17
  252.8 9.8 %custom-call.58 = f32[1,1,128,128]{2,3,1,0:T(8,128)S(1)} custom-call(f32[1,1,128,128]{3,2,1,0:T(8,128)S(1)} %get-tuple-element.131), custom_call_target="InvertDiagBlocksLowerTriangular" | custom-call | tf_op jit(solution)/shard_map/while/body/eval_jaxpr/jit(cholesky)/cholesky | solution.py:17
  263.4 11.7 %custom-call.59 = f32[1,128,128]{2,1,0:T(8,128)S(1)} custom-call(f32[1,128,128]{2,1,0:T(8,128)S(1)} %cholesky.306), custom_call_target="Cholesky" | custom-call | tf_op jit(solution)/shard_map/while/body/eval_jaxpr/jit(cholesky)/cholesky | solution.py:17
  275.4 10.0 %custom-call.60 = f32[1,1,128,128]{2,3,1,0:T(8,128)S(1)} custom-call(f32[1,1,128,128]{3,2,1,0:T(8,128)S(1)} %get-tuple-element.129), custom_call_target="InvertDiagBlocksLowerTriangular" | custom-call | tf_op jit(solution)/shard_map/while/body/eval_jaxpr/jit(cholesky)/cholesky | solution.py:17
  285.7 0.6 fusion.18
  286.3 11.7 %custom-call.61 = f32[1,128,128]{2,1,0:T(8,128)S(1)} custom-call(f32[1,128,128]{2,1,0:T(8,128)S(1)} %cholesky.311), custom_call_target="Cholesky" | custom-call | tf_op jit(solution)/shard_map/while/body/eval_jaxpr/jit(cholesky)/cholesky | solution.py:17
  298.2 9.8 %custom-call.62 = f32[1,1,128,128]{2,3,1,0:T(8,128)S(1)} custom-call(f32[1,1,128,128]{3,2,1,0:T(8,128)S(1)} %get-tuple-element.127), custom_call_target="InvertDiagBlocksLowerTriangular" | custom-call | tf_op jit(solution)/shard_map/while/body/eval_jaxpr/jit(cholesky)/cholesky | solution.py:17
  308.8 11.9 %custom-call.63 = f32[1,128,128]{2,1,0:T(8,128)S(1)} custom-call(f32[1,128,128]{2,1,0:T(8,128)S(1)} %fusion.21), custom_call_target="Cholesky" | custom-call | tf_op jit(solution)/shard_map/while/body/eval_jaxpr/jit(cholesky)/cholesky | solution.py:17
  320.8 0.6 compare_reduce_fusion.2
  321.5 0.7 compare_reduce_fusion.1
  322.1 0.7 compare_reduce_fusion.3
  325.5 8.1 %while.1 = (s32[]{:T(128)}, f32[1,512,512]{1,2,0:T(8,128)S(1)}, s32[4,2]{0,1:T(2,128)S(1)}, f32[4,1,128,128]{3,2,1,0:T(8,128)S(1)}, s32[]{:T(128)}) while((s32[]{:T(128)}, f32[1,512,512]{1,2,0:T(8,128)S(1)}, s32[4,2]{0,1:T(2,128)S(1)}, f32[4,1,128,128]{3,2,1,0:T(8,128)S(1)}, s32[]{:T(128)}) %tuple.57), condition=%wide.while_cond, body=%wide.while_body.sunk | while | flops 2 | bytes 393333 | solution.py:20
  325.6 0.5 fusion.127
  326.1 1.3 constant_dynamic-slice_fusion.11
  327.7 0.5 fusion.127
  328.2 1.3 constant_dynamic-slice_fusion.11
  329.7 0.5 fusion.127
  330.2 1.3 constant_dynamic-slice_fusion.11
  331.7 0.5 fusion.127
  332.2 1.3 constant_dynamic-slice_fusion.11
  333.7 39.3 %custom-call.64 = f32[1,4,128,128]{2,3,1,0:T(8,128)S(1)} custom-call(f32[1,4,128,128]{3,2,1,0:T(8,128)S(1)} %bitcast.370), custom_call_target="InvertDiagBlocksLowerTriangular" | custom-call | tf_op jit(solution)/shard_map/while/body/eval_jaxpr/vmap(jit(_cho_solve))/triangular_solve | solution.py:20
  373.0 1.8 fusion.107
  374.8 0.7 copy.187
  375.7 0.8 fusion.106
  376.5 0.8 fusion.72
  380.3 0.7 fusion.70
  381.0 0.7 dynamic-slice_convert_fusion
  382.4 74.5 %all-gather.2.cloned.1.call-done = bf16[64,512,16]{1,2,0:T(8,128)(2,1)} async-done(((bf16[1,512,16]{1,2,0:T(8,128)(2,1)}), bf16[64,512,16]{1,2,0:T(8,128)(2,1)}) %all-gather.2.cloned.1.call-update) | async-done | bytes 1048592 | tf_op jit(solution)/shard_map/all_gather | solution.py:91
  456.8 1.0 slice.263
  457.9 1.5 fusion.111
  459.4 0.5 fusion.9
  459.9 0.9 copy.188
  460.8 4.8 all-to-all-start
  466.2 4.4 all-to-all-done
  471.8 1.3 fusion.13
  473.4 3.5 psum.29
  476.9 29.2 %psum.30 = f32[20,440]{1,0:T(8,128)S(1)} all-reduce(f32[20,440]{1,0:T(8,128)S(1)} %psum.29), channel_id=1, replica_groups=mesh['x'=4,'z'=8,'c'=2,'blk'=4] {'z'}, use_global_device_ids=true, to_apply=%region_16.17 | all-reduce | flops 8800 | bytes 70400 | tf_op jit(solution)/shard_map/psum | solution.py:27
  506.1 16.2 %psum.31 = f32[20,440]{1,0:T(8,128)S(1)} all-reduce(f32[20,440]{1,0:T(8,128)S(1)} %psum.30), channel_id=1, replica_groups=mesh['x'=4,'z'=8,'c'=2,'blk'=4] {'x'}, use_global_device_ids=true, to_apply=%region_17.18 | all-reduce | flops 8800 | bytes 70400 | tf_op jit(solution)/shard_map/psum | solution.py:27
  522.6 0.6 copy.199
  523.2 0.8 gather_fusion.1
  524.2 0.6 fusion.96
  524.8 0.6 add_rsqrt_fusion
  527.4 36.7 %custom-call.65 = f32[20,20,20]{2,1,0:T(8,128)S(1)} custom-call(f32[20,20,20]{2,1,0:T(8,128)S(1)} %fusion.44), custom_call_target="Cholesky" | custom-call | tf_op jit(solution)/shard_map/jit(cholesky)/cholesky | solution.py:17
  564.4 30.9 %custom-call.66 = f32[20,1,20,20]{2,3,1,0:T(8,128)S(1)} custom-call(f32[20,1,20,20]{3,2,1,0:T(8,128)S(1)} %select_bitcast_fusion), custom_call_target="InvertDiagBlocksLowerTriangular" | custom-call | tf_op jit(solution)/shard_map/vmap(jit(_cho_solve))/triangular_solve | solution.py:20
  595.7 0.5 fusion.40
  596.6 0.7 copy.213
  597.3 0.5 fusion.54
  598.4 0.6 add_rsqrt_fusion.2
  599.0 0.7 multiply_bitcast_fusion.1
  (140 shorter events, 13.1 us)
Async XLA Ops:
  7.2 214.3 %all-reduce.3.cloned.1.call-start = ((), (), s32[]{:S(2)}) async-start(), calls=%async_computation.1 | async-start | bytes 13721600 | tf_op jit(solution)/shard_map/psum | solution.py:41
  16.3 0.7 copy-start.4
  16.4 440.5 %all-gather.2.cloned.1.call-start = ((), (), s32[]{:S(2)}) async-start(), calls=%async_computation.2 | async-start | bytes 1064960 | tf_op jit(solution)/shard_map/all_gather | solution.py:91
  373.0 86.4 %copy-start = (bf16[640,512]{1,0:T(8,128)(2,1)S(1)}, bf16[640,512]{1,0:T(8,128)(2,1)}, u32[]{:S(2)}) copy-start(bf16[640,512]{1,0:T(8,128)(2,1)} %param.4) | copy-start | bytes 1966084
  375.6 83.8 %copy-start.1 = (f32[640,5]{0,1:T(8,128)S(1)}, f32[640,5]{0,1:T(8,128)}, u32[]{:S(2)}) copy-start(f32[640,5]{0,1:T(8,128)} %get-tuple-element.137) | copy-start | bytes 38404
  378.1 92.7 %copy-start.2 = (s32[640]{0:T(1024)S(1)}, s32[640]{0:T(1024)}, u32[]{:S(2)}) copy-start(s32[640]{0:T(1024)} %param.6) | copy-start | bytes 7684
  380.1 91.7 %copy-start.3 = (f32[640,5]{0,1:T(8,128)S(1)}, f32[640,5]{0,1:T(8,128)}, u32[]{:S(2)}) copy-start(f32[640,5]{0,1:T(8,128)} %get-tuple-element.136) | copy-start | bytes 38404
  460.8 9.8 %all-to-all-start = ((f32[1,5,16,640]{3,0,1,2:T(1,128)}), f32[1,5,16,640]{3,0,1,2:T(1,128)S(1)}, u32[]{:S(2)}, u32[]{:S(2)}) async-start(f32[1,5,16,640]{3,0,1,2:T(1,128)} %copy.188), calls=%async_computation | async-start | bytes 409600 | tf_op jit(solution)/shard_map/all_to_all | solution.py:102
Sparse Core Ops, SparseCore 0:
  16.5 204.9 all-reduce.2
  381.1 75.6 all-gather.1
where the time goes:
time: 611 us; the launch traced here: 607 us
  waiting for transfers between devices  283 us (46%)
  other arithmetic  210 us (34%)
  blocking collectives  48.9 us (8%)
  local copies, waits for them, and re-layouts  24 us (4%)
  between operations  19.3 us (3%)
  matrix products  16.7 us (3%)
    psum x1, waiting for transfers between devices, shards(): stats = lax.psum(stats, SAMP)  204 us
    another operation x18, other arithmetic, solve_batch(): factors = jnp.linalg.cholesky(systems)  116 us
    all_gather x1, waiting for transfers between devices, shards(): collected = lax.all_gather(owned, SAMP, axis=0, tiled=True)  74.5 us
    another operation x6, other arithmetic, solve_single(): return jax.scipy.linalg.cho_solve((factor, True), right_side)  70.5 us
    psum x3, blocking collectives, psum_tree(): value = lax.psum(value, name)  48.9 us
  transfers between devices with their start and end apart: 3, of which 3 were waited for; matrix products, arithmetic and copies ran while one was open for 0% of the time, Pallas kernels for 0%

commit v1 on v0

--- a/solution.py
+++ b/solution.py
@@ -88,7 +88,9 @@
         return (scale[:, None] * beta).astype(jnp.bfloat16)
 
     owned = lax.map(solve_own, jnp.arange(per_device, dtype=jnp.int32))
-    collected = lax.all_gather(owned, SAMP, axis=0, tiled=True)
+    collected = jnp.concatenate(
+        lax.all_to_all(jnp.stack([owned] * lax.axis_size(SAMP)), SAMP, 0, 0), axis=0
+    )
     coef = collected[:systems_count].reshape(FOLDS, SHRINK, width, traits_count)
     coef_flat = coef.transpose(2, 0, 1, 3).reshape(width, FOLDS * SHRINK * traits_count)
     shift = jnp.einsum("v,klvt->klt", mean, coef.astype(jnp.float32), precision=HIGH)

time: 611 us -> 573 us (0.938)
  waiting for transfers between devices: 283 us -> 235 us
  starting transfers between devices: 4.9 us -> 13 us
    all_gather x1 -> x0, waiting for transfers between devices: 74.5 us -> none  [shards(): collected = lax.all_gather(owned, SAMP, axis=0, tiled=True)]
    all_to_all x0 -> x1, waiting for transfers between devices: none -> 26.8 us  [shards(): lax.all_to_all(jnp.stack([owned] * lax.axis_size(SAMP)), SAMP, 0, 0)]
    all_to_all x0 -> x1, starting transfers between devices: none -> 8.14 us  [shards(): lax.all_to_all(jnp.stack([owned] * lax.axis_size(SAMP)), SAMP, 0, 0)]
where the time goes in v1:
time: 573 us; the launch traced here: 568 us
  waiting for transfers between devices  235 us (41%)
  other arithmetic  209 us (36%)
  blocking collectives  49.3 us (9%)
  local copies, waits for them, and re-layouts  26 us (5%)
  between operations  19.3 us (3%)
  matrix products  16.7 us (3%)
  starting transfers between devices  13 us (2%)
    psum x1, waiting for transfers between devices, shards(): stats = lax.psum(stats, SAMP)  204 us
    another operation x18, other arithmetic, solve_batch(): factors = jnp.linalg.cholesky(systems)  116 us
    another operation x6, other arithmetic, solve_single(): return jax.scipy.linalg.cho_solve((factor, True), right_side)  71.3 us
    psum x3, blocking collectives, psum_tree(): value = lax.psum(value, name)  49.3 us
    all_to_all x1, waiting for transfers between devices, shards(): lax.all_to_all(jnp.stack([owned] * lax.axis_size(SAMP)), SAMP, 0, 0)  26.8 us
  transfers between devices with their start and end apart: 3, of which 3 were waited for; matrix products, arithmetic and copies ran while one was open for 0% of the time, Pallas kernels for 0%

profile of v1, /device:TPU:8, one launch (start us, length us, event | category | flops | bytes accessed | tf_op | source)
XLA Modules:
  0.0 568.5 jit_solution(6021007631954418304)
XLA Ops:
  7.2 1.4 copy.177
  8.6 0.7 convert_bitcast_fusion
  9.3 0.9 pad_maximum_fusion
  10.2 5.5 fusion.2
  15.8 0.6 copy-done.2
  16.4 0.6 fusion.102
  17.0 203.9 %all-reduce.3.cloned.1.call-done = f32[5,529,529]{1,2,0:T(8,128)} async-done(((f32[5,529,529]{1,2,0:T(8,128)}), f32[5,529,529]{1,2,0:T(8,128)}) %all-reduce.3.cloned.1.call-update) | async-done | bytes 5596836 | tf_op jit(solution)/shard_map/psum | solution.py:41
  220.9 1.5 slice_reduce_fusion.1
  222.4 0.5 constant_dynamic-slice_fusion.5
  222.9 0.9 fusion.113
  225.0 6.1 %fusion.114 = (f32[5,512,512]{1,2,0:T(8,128)}, f32[512,512]{0,1:T(8,128)S(1)}) fusion(f32[5,529,529]{1,2,0:T(8,128)} %all-reduce.3.cloned.1.call-done), kind=kLoop, calls=%fused_computation.229 | loop fusion | flops 1048576 | bytes 11534336 | tf_op jit(solution)/shard_map/slice | solution.py:42
  231.1 5.1 gather_fusion
  236.1 0.6 broadcast_multiply_fusion.3
  236.8 0.6 add_rsqrt_fusion.1
  237.4 2.4 fusion.35
  240.3 11.7 %custom-call.57 = f32[1,128,128]{2,1,0:T(8,128)S(1)} custom-call(f32[1,128,128]{2,1,0:T(8,128)S(1)} %cholesky.302), custom_call_target="Cholesky" | custom-call | tf_op jit(solution)/shard_map/while/body/eval_jaxpr/jit(cholesky)/cholesky | solution.py:17
  252.2 9.8 %custom-call.58 = f32[1,1,128,128]{2,3,1,0:T(8,128)S(1)} custom-call(f32[1,1,128,128]{3,2,1,0:T(8,128)S(1)} %get-tuple-element.131), custom_call_target="InvertDiagBlocksLowerTriangular" | custom-call | tf_op jit(solution)/shard_map/while/body/eval_jaxpr/jit(cholesky)/cholesky | solution.py:17
  262.8 11.7 %custom-call.59 = f32[1,128,128]{2,1,0:T(8,128)S(1)} custom-call(f32[1,128,128]{2,1,0:T(8,128)S(1)} %cholesky.306), custom_call_target="Cholesky" | custom-call | tf_op jit(solution)/shard_map/while/body/eval_jaxpr/jit(cholesky)/cholesky | solution.py:17
  274.8 10.0 %custom-call.60 = f32[1,1,128,128]{2,3,1,0:T(8,128)S(1)} custom-call(f32[1,1,128,128]{3,2,1,0:T(8,128)S(1)} %get-tuple-element.129), custom_call_target="InvertDiagBlocksLowerTriangular" | custom-call | tf_op jit(solution)/shard_map/while/body/eval_jaxpr/jit(cholesky)/cholesky | solution.py:17
  285.1 0.6 fusion.18
  285.7 11.7 %custom-call.61 = f32[1,128,128]{2,1,0:T(8,128)S(1)} custom-call(f32[1,128,128]{2,1,0:T(8,128)S(1)} %cholesky.311), custom_call_target="Cholesky" | custom-call | tf_op jit(solution)/shard_map/while/body/eval_jaxpr/jit(cholesky)/cholesky | solution.py:17
  297.6 9.8 %custom-call.62 = f32[1,1,128,128]{2,3,1,0:T(8,128)S(1)} custom-call(f32[1,1,128,128]{3,2,1,0:T(8,128)S(1)} %get-tuple-element.127), custom_call_target="InvertDiagBlocksLowerTriangular" | custom-call | tf_op jit(solution)/shard_map/while/body/eval_jaxpr/jit(cholesky)/cholesky | solution.py:17
  308.2 11.9 %custom-call.63 = f32[1,128,128]{2,1,0:T(8,128)S(1)} custom-call(f32[1,128,128]{2,1,0:T(8,128)S(1)} %fusion.21), custom_call_target="Cholesky" | custom-call | tf_op jit(solution)/shard_map/while/body/eval_jaxpr/jit(cholesky)/cholesky | solution.py:17
  320.2 0.6 compare_reduce_fusion.2
  320.9 0.7 compare_reduce_fusion.1
  321.5 0.7 compare_reduce_fusion.3
  324.9 10.5 %while.1 = (s32[]{:T(128)}, f32[1,512,512]{1,2,0:T(8,128)S(1)}, s32[4,2]{0,1:T(2,128)S(1)}, f32[4,1,128,128]{3,2,1,0:T(8,128)}, s32[]{:T(128)}) while((s32[]{:T(128)}, f32[1,512,512]{1,2,0:T(8,128)S(1)}, s32[4,2]{0,1:T(2,128)S(1)}, f32[4,1,128,128]{3,2,1,0:T(8,128)}, s32[]{:T(128)}) %tuple.57), condition=%wide.while_cond, body=%wide.while_body.sunk | while | flops 2 | bytes 393333 | solution.py:20
  325.0 0.5 fusion.130
  325.5 1.3 constant_dynamic-slice_fusion.11
  326.9 0.6 bitcast_dynamic-update-slice_fusion.2
  327.6 0.5 fusion.130
  328.2 1.3 constant_dynamic-slice_fusion.11
  329.6 0.6 bitcast_dynamic-update-slice_fusion.2
  330.3 0.5 fusion.130
  330.8 1.3 constant_dynamic-slice_fusion.11
  332.2 0.6 bitcast_dynamic-update-slice_fusion.2
  332.9 0.5 fusion.130
  333.4 1.3 constant_dynamic-slice_fusion.11
  334.8 0.6 bitcast_dynamic-update-slice_fusion.2
  335.4 40.1 %custom-call.64 = f32[1,4,128,128]{2,3,1,0:T(8,128)S(1)} custom-call(f32[1,4,128,128]{3,2,1,0:T(8,128)} %bitcast.371), custom_call_target="InvertDiagBlocksLowerTriangular" | custom-call | tf_op jit(solution)/shard_map/while/body/eval_jaxpr/vmap(jit(_cho_solve))/triangular_solve | solution.py:20
  375.6 1.8 fusion.112
  377.6 0.9 fusion.111
  381.6 1.1 stack.2
  382.7 8.1 %all-to-all-start = ((bf16[64,1,512,16]{2,3,1,0:T(8,128)(2,1)}), bf16[64,1,512,16]{2,3,1,0:T(8,128)(2,1)S(1)}, u32[]{:S(2)}, u32[]{:S(2)}) async-start(bf16[64,1,512,16]{2,3,1,0:T(8,128)(2,1)} %stack.2), calls=%async_computation | async-start | bytes 2097152 | tf_op jit(solution)/shard_map/all_to_all | solution.py:92
  390.9 0.7 dynamic-slice_convert_fusion
  392.2 26.8 %all-to-all-done = bf16[64,1,512,16]{2,3,1,0:T(8,128)(2,1)S(1)} async-done(((bf16[64,1,512,16]{2,3,1,0:T(8,128)(2,1)}), bf16[64,1,512,16]{2,3,1,0:T(8,128)(2,1)S(1)}, u32[]{:S(2)}, u32[]{:S(2)}) %all-to-all-start) | async-done | bytes 1048608 | tf_op jit(solution)/shard_map/all_to_all | solution.py:92
  419.0 1.5 fusion.40
  420.5 0.5 fusion.9
  421.0 0.9 copy.189
  421.9 4.8 all-to-all-start.1
  427.4 4.6 all-to-all-done.1
  433.2 1.3 fusion.13
  434.8 3.5 psum.29
  438.3 28.6 %psum.30 = f32[20,440]{1,0:T(8,128)S(1)} all-reduce(f32[20,440]{1,0:T(8,128)S(1)} %psum.29), channel_id=1, replica_groups=mesh['x'=4,'z'=8,'c'=2,'blk'=4] {'z'}, use_global_device_ids=true, to_apply=%region_16.17 | all-reduce | flops 8800 | bytes 70400 | tf_op jit(solution)/shard_map/psum | solution.py:27
  466.9 17.1 %psum.31 = f32[20,440]{1,0:T(8,128)S(1)} all-reduce(f32[20,440]{1,0:T(8,128)S(1)} %psum.30), channel_id=1, replica_groups=mesh['x'=4,'z'=8,'c'=2,'blk'=4] {'x'}, use_global_device_ids=true, to_apply=%region_17.18 | all-reduce | flops 8800 | bytes 70400 | tf_op jit(solution)/shard_map/psum | solution.py:27
  484.3 0.6 copy.200
  484.9 0.8 gather_fusion.1
  485.8 0.6 fusion.101
  486.5 0.6 add_rsqrt_fusion
  489.1 36.7 %custom-call.65 = f32[20,20,20]{2,1,0:T(8,128)S(1)} custom-call(f32[20,20,20]{2,1,0:T(8,128)S(1)} %fusion.46), custom_call_target="Cholesky" | custom-call | tf_op jit(solution)/shard_map/jit(cholesky)/cholesky | solution.py:17
  526.0 30.9 %custom-call.66 = f32[20,1,20,20]{2,3,1,0:T(8,128)S(1)} custom-call(f32[20,1,20,20]{3,2,1,0:T(8,128)S(1)} %select_bitcast_fusion), custom_call_target="InvertDiagBlocksLowerTriangular" | custom-call | tf_op jit(solution)/shard_map/vmap(jit(_cho_solve))/triangular_solve | solution.py:20
  558.3 0.7 copy.214
  560.1 0.6 add_rsqrt_fusion.2
  560.7 0.7 multiply_bitcast_fusion.1
  (136 shorter events, 14.3 us)
Async XLA Ops:
  7.2 213.7 %all-reduce.3.cloned.1.call-start = ((), (), s32[]{:S(2)}) async-start(), calls=%async_computation.2 | async-start | bytes 13721600 | tf_op jit(solution)/shard_map/psum | solution.py:41
  15.7 0.7 copy-start.2
  377.5 43.0 %copy-start = (bf16[640,512]{1,0:T(8,128)(2,1)S(1)}, bf16[640,512]{1,0:T(8,128)(2,1)}, u32[]{:S(2)}) copy-start(bf16[640,512]{1,0:T(8,128)(2,1)} %param.4) | copy-start | bytes 1966084
  382.7 49.5 %copy-start.1 = (s32[640]{0:T(1024)S(1)}, s32[640]{0:T(1024)}, u32[]{:S(2)}) copy-start(s32[640]{0:T(1024)} %param.6) | copy-start | bytes 7684
  382.7 36.3 %all-to-all-start = ((bf16[64,1,512,16]{2,3,1,0:T(8,128)(2,1)}), bf16[64,1,512,16]{2,3,1,0:T(8,128)(2,1)S(1)}, u32[]{:S(2)}, u32[]{:S(2)}) async-start(bf16[64,1,512,16]{2,3,1,0:T(8,128)(2,1)} %stack.2), calls=%async_computation | async-start | bytes 2097152 | tf_op jit(solution)/shard_map/all_to_all | solution.py:92
  421.9 10.0 %all-to-all-start.1 = ((f32[1,5,16,640]{3,0,1,2:T(1,128)}), f32[1,5,16,640]{3,0,1,2:T(1,128)S(1)}, u32[]{:S(2)}, u32[]{:S(2)}) async-start(f32[1,5,16,640]{3,0,1,2:T(1,128)} %copy.189), calls=%async_computation.1 | async-start | bytes 409600 | tf_op jit(solution)/shard_map/all_to_all | solution.py:104
Sparse Core Ops, SparseCore 0:
  15.9 204.9 all-reduce.2
